TPU v7x, 512 devices: a whole 4x8x8 slice. The times are simulated.
512 devices in a mesh: ctx: 64 (over z, y), section: 2 (over x_hi), dp: 4 (over x_lo, core).
Axes of the slice: x: 4 (x_hi: 2, x_lo: 2; x = x_hi * 2 + x_lo), y: 8, z: 8, core: 2. Of those that a mesh axis runs over, the one named last changes fastest.
Arguments:
- query_vectors: bfloat16 [4, 8192, 1792], P('dp', 'ctx', 'section'), may hold values from -16 to 16
- key_vectors: bfloat16 [4, 8192, 256], P('dp', 'ctx', 'section'), may hold values from -16 to 16
- value_vectors: bfloat16 [4, 8192, 256], P('dp', 'ctx', 'section'), may hold values from -6 to 6
- grad_output: bfloat16 [4, 8192, 1792], P('dp', 'ctx', 'section'), may hold values from -24 to 24
- output_dots: float32 [4, 14, 8192], P('dp', 'section', 'ctx'), may hold values from -12 to 12
- frame_ids: int32 [4, 8192], P('dp'), may hold values from 0 to 63, never falling along the last dimension, each value on 1 to 256 neighbouring positions
- visual_rows: int32 [4, 64, 32], P('dp', 'ctx'), may hold values from 0 to 127, as said below
- shuffle_source: int32 [4, 128, 64], P('dp', ('ctx', 'section')), may hold values from 0 to 63, each once within a row
- qkv_weight: bfloat16 [2304, 3584], P(None, ('section', 'dp')), may hold values from -0.125 to 0.125
- projector_weight: bfloat16 [3584, 2560], P(('section', 'dp')), may hold values from -0.09375 to 0.09375
Outputs:
- grad_keys: bfloat16 [4, 8192, 256], P('dp', 'ctx', 'section')
- grad_values: bfloat16 [4, 8192, 256], P('dp', 'ctx', 'section')
- patch_grads: bfloat16 [4, 8192, 640], P('dp', ('ctx', 'section'))
Inputs may be any that keep to these rules, and one draw needn't show every extreme that they name: `frame_ids`: frame numbers never fall along a sequence; a frame holds 1 to 256 tokens. `visual_rows`: each block of 128 tokens lists 32 distinct positions in increasing order. `shuffle_source`: each row is a permutation.
All inputs are finite; a program needn't handle non-finite values.
Results may differ from a plain program's by a relative error of at most 0.014.
Values may be sent and summed in bfloat16 or wider, within the bound.
No kernel may reach another device: no remote copies, remote signals or barrier semaphores. Data moves between devices by JAX's collectives and lax.ppermute only.
A program may use at most 128 MiB of HBM per device.

v0:
```python
import math
import jax
import jax.numpy as jnp
from jax import lax
from jax.sharding import PartitionSpec as P

HEAD_DIM = 128
GROUP = 7
MASKED = -1e30


def shards(
    query_vectors,
    key_vectors,
    value_vectors,
    grad_output,
    output_dots,
    frame_ids,
    visual_rows,
    shuffle_source,
    qkv_weight,
    projector_weight,
):
    position = lax.axis_index("ctx")
    local_rows = query_vectors.shape[1]
    scale_factor = 1.0 / math.sqrt(HEAD_DIM)
    query_heads = query_vectors[0].reshape(local_rows, GROUP, HEAD_DIM)
    grad_heads = grad_output[0].reshape(local_rows, GROUP, HEAD_DIM)
    corrections = output_dots[0]
    frame_line = frame_ids[0]
    seq_total = frame_line.shape[0]
    query_first = position * local_rows
    query_pos = query_first + jnp.arange(local_rows, dtype=jnp.int32)
    query_frames = lax.dynamic_slice_in_dim(frame_line, query_first, local_rows)
    own_pair = jnp.concatenate([key_vectors[0], value_vectors[0]], axis=1)
    all_pairs = lax.all_gather(own_pair, "ctx", axis=0, tiled=True)
    key_all = all_pairs[:, :HEAD_DIM]
    value_all = all_pairs[:, HEAD_DIM:]
    key_pos = jnp.arange(seq_total, dtype=jnp.int32)
    allowed = (key_pos[None, :] <= query_pos[:, None]) | (
        frame_line[None, :] == query_frames[:, None]
    )
    scores = (
        jnp.einsum("qhd,kd->hqk", query_heads, key_all, preferred_element_type=jnp.float32)
        * scale_factor
    )
    masked_scores = jnp.where(allowed[None], scores, MASKED)
    running = masked_scores.max(axis=-1)
    summed = jnp.exp(masked_scores - running[:, :, None]).sum(axis=-1)
    log_total = running + jnp.log(summed)
    probability = jnp.exp(jnp.where(allowed[None], scores - log_total[:, :, None], MASKED))
    probs_low = probability.astype(jnp.bfloat16)
    grad_probs = jnp.einsum(
        "qhd,kd->hqk", grad_heads, value_all, preferred_element_type=jnp.float32
    )
    grad_scores = (probability * (grad_probs - corrections[:, :, None])).astype(jnp.bfloat16)
    grad_query = (
        jnp.einsum("hqk,kd->qhd", grad_scores, key_all, preferred_element_type=jnp.float32)
        * scale_factor
    )
    key_part = (
        jnp.einsum("hqk,qhd->kd", grad_scores, query_heads, preferred_element_type=jnp.float32)
        * scale_factor
    )
    value_part = jnp.einsum(
        "hqk,qhd->kd", probs_low, grad_heads, preferred_element_type=jnp.float32
    )
    summed_grads = lax.psum_scatter(
        jnp.concatenate([key_part, value_part], axis=1), "ctx", scatter_dimension=0, tiled=True
    )
    grad_keys_low = summed_grads[:, :HEAD_DIM].astype(jnp.bfloat16)
    grad_values_low = summed_grads[:, HEAD_DIM:].astype(jnp.bfloat16)
    grad_query_low = grad_query.astype(jnp.bfloat16).reshape(local_rows, GROUP * HEAD_DIM)
    visual_picks = visual_rows[0, 0]
    chosen = jnp.concatenate(
        [grad_query_low[visual_picks], grad_keys_low[visual_picks], grad_values_low[visual_picks]],
        axis=1,
    )
    everyone = lax.all_gather(chosen[None], ("section", "dp"), axis=0, tiled=True)
    groups = lax.axis_size("section")
    replicas = lax.axis_size("dp")
    half_rows = visual_picks.shape[0] // 2
    width_in = chosen.shape[1]
    arranged = (
        everyone.reshape(groups, replicas, 2, half_rows, width_in)
        .transpose(2, 1, 3, 0, 4)
        .reshape(2 * replicas * half_rows, groups * width_in)
    )
    visual_grad = jnp.dot(arranged, qkv_weight, preferred_element_type=jnp.float32).astype(
        jnp.bfloat16
    )
    shuffled = lax.psum_scatter(
        jnp.dot(visual_grad, projector_weight, preferred_element_type=jnp.float32).astype(
            jnp.bfloat16
        ),
        ("section", "dp"),
        scatter_dimension=0,
        tiled=True,
    ).astype(jnp.float32)
    slot_rows = shuffled.reshape(half_rows * 4, projector_weight.shape[1] // 4)
    patches = slot_rows[shuffle_source[0, 0]].astype(jnp.bfloat16)
    return (grad_keys_low[None], grad_values_low[None], patches[None])


def solution(mesh):
    placed = (
        P("dp", "ctx", "section"),
        P("dp", "ctx", "section"),
        P("dp", "ctx", "section"),
        P("dp", "ctx", "section"),
        P("dp", "section", "ctx"),
        P("dp", None),
        P("dp", "ctx", None),
        P("dp", ("ctx", "section"), None),
        P(None, ("section", "dp")),
        P(("section", "dp"), None),
    )
    return jax.shard_map(
        shards,
        mesh=mesh,
        in_specs=placed,
        out_specs=(
            P("dp", "ctx", "section"),
            P("dp", "ctx", "section"),
            P("dp", ("ctx", "section"), None),
        ),
        check_vma=False,
    )
```

profile of v0, /device:TPU:8, one launch (start us, length us, event | category | flops | bytes accessed | tf_op | source)
XLA Modules:
  0.0 487.8 jit_solution(14910348359824243187)
XLA Ops:
  7.2 1.6 pad_maximum_fusion.2
  8.9 1.8 copy.28
  10.6 1.8 copy.26
  12.4 0.7 copy.50
  13.1 0.7 dynamic-slice_bitcast_fusion
  13.8 4.3 fusion.13
  18.0 85.1 %all-gather.3.cloned.1.call-done = bf16[8192,256]{1,0:T(8,128)(2,1)} async-done(((bf16[128,256]{1,0:T(8,128)(2,1)}), bf16[8192,256]{1,0:T(8,128)(2,1)}) %all-gather.3.cloned.1.call-update) | async-done | bytes 4194320 | tf_op jit(solution)/shard_map/all_gather | solution.py:36
  103.1 13.1 %fusion.4 = (f32[7,128]{1,0:T(8,128)S(1)}, f32[8192,128,7]{1,0,2:T(8,128)}) fusion(pred[128,8192]{0,1:T(8,128)(4,1)S(1)} %fusion.13, bf16[128,7,128]{0,2,1:T(8,128)(2,1)} %bitcast.90, bf16[8192,256]{1,0:T(8,128)(2,1)} %all-gather.3.cloned.1.call-done), kind=kOutput, calls=%fused_computation.12 | convolution fusion | flops 1901067392 | bytes 32738816 | tf_op jit(solution)/shard_map/qhd,kd->hqk/dot_general | solution.py:44
  116.2 12.7 %exponential_reduce_fusion = f32[7,128]{1,0:T(8,128)S(1)} fusion(f32[8192,128,7]{1,0,2:T(8,128)} %get-tuple-element.14, f32[7,128]{1,0:T(8,128)S(1)} %get-tuple-element.13, pred[128,8192]{0,1:T(8,128)(4,1)S(1)} %fusion.13), kind=kLoop, calls=%fused_computation.11 | loop fusion | flops 29359232 | bytes 30415872 | tf_op jit(solution)/shard_map/reduce_sum | solution.py:49
  129.0 13.4 %fusion.9 = f32[8192,128]{0,1:T(8,128)S(1)} fusion(bf16[128,7,128]{0,2,1:T(8,128)(2,1)S(1)} %bitcast.92, f32[8192,128,7]{1,0,2:T(8,128)} %get-tuple-element.14, f32[7,128]{1,0:T(8,128)S(1)} %log_add_fusion, pred[128,8192]{0,1:T(8,128)(4,1)S(1)} %fusion.13), kind=kOutput, calls=%fused_computation.17 | convolution fusion | flops 1908408320 | bytes 34835968 | tf_op jit(solution)/shard_map/hqk,qhd->kd/dot_general | solution.py:65
  142.4 19.4 %fusion.1 = bf16[7,128,8192]{1,2,0:T(8,128)(2,1)} fusion(f32[8192,128,7]{1,0,2:T(8,128)} %get-tuple-element.14, bf16[128,7,128]{0,2,1:T(8,128)(2,1)S(1)} %bitcast.93, f32[7,128]{1,0:T(8,128)S(1)} %bitcast.98, f32[7,128]{1,0:T(8,128)S(1)} %log_add_fusion, pred[128,8192]{0,1:T(8,128)(4,1)S(1)} %fusion.13, bf16[8192,256]{1,0:T(8,128)(2,1)S(1)} %copy-done.1), kind=kOutput, calls=%fused_computation.6 | convolution fusion | flops 1923088384 | bytes 47423488 | tf_op jit(solution)/shard_map/qhd,kd->hqk/dot_general | solution.py:53
  161.8 9.9 %fusion.12 = f32[8192,128]{0,1:T(8,128)S(1)} fusion(bf16[7,128,8192]{1,2,0:T(8,128)(2,1)} %fusion.1, bf16[128,7,128]{0,2,1:T(8,128)(2,1)S(1)} %bitcast.91), kind=kOutput, calls=%fused_computation.18 | convolution fusion | flops 1880096768 | bytes 19103744 | tf_op jit(solution)/shard_map/hqk,qhd->kd/dot_general | solution.py:62
  171.7 4.1 pad_maximum_fusion
  175.9 0.0 reduce-scatter.5.cloned.1.call-start
  176.0 8.2 %fusion.17 = bf16[128,7,128]{2,0,1:T(8,128)(2,1)S(1)} fusion(bf16[7,128,8192]{1,2,0:T(8,128)(2,1)} %fusion.1, bf16[8192,256]{1,0:T(8,128)(2,1)} %all-gather.3.cloned.1.call-done), kind=kOutput, calls=%fused_computation.28 | convolution fusion | flops 1879277568 | bytes 17006592 | tf_op jit(solution)/shard_map/hqk,kd->qhd/dot_general | solution.py:58
  184.2 0.2 copy.34
  184.3 0.6 gather_fusion
  185.0 240.0 %reduce-scatter.3.cloned.1.call-done = f32[128,256]{0,1:T(8,128)} async-done(((f32[8192,256]{0,1:T(8,128)}), f32[128,256]{0,1:T(8,128)}) %reduce-scatter.3.cloned.1.call-update) | async-done | bytes 131088 | tf_op jit(solution)/shard_map/reduce_scatter | solution.py:68
  424.9 0.9 convert.5
  425.9 0.1 copy.36
  426.0 0.6 gather_fusion.2
  426.6 0.1 copy.35
  426.7 0.6 gather_fusion.1
  427.3 13.5 %all-gather = bf16[256,1152]{1,0:T(8,128)(2,1)S(1)} all-gather(bf16[32,1152]{1,0:T(8,128)(2,1)S(1)} %pad_maximum_fusion.1), channel_id=2, replica_groups=mesh['ctx'=64,'section'=2,'dp'=4] {'section','dp'}, dimensions={0}, use_global_device_ids=true | all-gather | bytes 663552 | tf_op jit(solution)/shard_map/all_gather | solution.py:79
  440.8 0.6 copy.37
  441.4 0.1 copy.48
  441.5 3.7 convolution_convert_fusion
  445.3 0.7 copy.38
  446.0 0.7 copy.39
  446.8 32.2 %reduce-scatter.5.cloned.1.call-done = bf16[16,2560]{1,0:T(8,128)(2,1)} async-done(((bf16[128,2560]{1,0:T(8,128)(2,1)}), bf16[16,2560]{1,0:T(8,128)(2,1)}) %reduce-scatter.5.cloned.1.call-update) | async-done | bytes 81936 | tf_op jit(solution)/shard_map/reduce_scatter | solution.py:92
  479.0 0.9 reshape.155
  480.0 1.3 gather_fusion.3
  (25 shorter events, 0.2 us)
Async XLA Ops:
  7.2 434.3 %copy-start = (bf16[448,2560]{1,0:T(8,128)(2,1)S(1)}, bf16[448,2560]{1,0:T(8,128)(2,1)}, u32[]{:S(2)}) copy-start(bf16[448,2560]{1,0:T(8,128)(2,1)} %param.19) | copy-start | bytes 6881284
  7.2 95.9 %all-gather.3.cloned.1.call-start = ((), (), s32[]{:S(2)}) async-start(), calls=%async_computation.2 | async-start | bytes 4259840 | tf_op jit(solution)/shard_map/all_gather | solution.py:36
  8.8 416.1 %reduce-scatter.3.cloned.1.call-start = ((), (), s32[]{:S(2)}) async-start(), calls=%async_computation.3 | async-start | bytes 8519680 | tf_op jit(solution)/shard_map/reduce_scatter | solution.py:68
  116.2 12.7 %copy-start.3 = (bf16[1,128,896]{1,2,0:T(8,128)(2,1)S(1)}, bf16[1,128,896]{1,2,0:T(8,128)(2,1)}, u32[]{:S(2)}) copy-start(bf16[1,128,896]{1,2,0:T(8,128)(2,1)} %copy.28) | copy-start | bytes 688132
  129.0 13.4 %copy-start.1 = (bf16[8192,256]{1,0:T(8,128)(2,1)S(1)}, bf16[8192,256]{1,0:T(8,128)(2,1)}, u32[]{:S(2)}) copy-start(bf16[8192,256]{1,0:T(8,128)(2,1)} %all-gather.3.cloned.1.call-done) | copy-start | bytes 12582916
  142.4 19.4 %copy-start.2 = (bf16[1,128,896]{1,2,0:T(8,128)(2,1)S(1)}, bf16[1,128,896]{1,2,0:T(8,128)(2,1)}, u32[]{:S(2)}) copy-start(bf16[1,128,896]{1,2,0:T(8,128)(2,1)} %copy.26) | copy-start | bytes 688132
  171.7 4.2 copy-start.4
  175.9 303.1 %reduce-scatter.5.cloned.1.call-start = ((), (), s32[]{:S(2)}) async-start(), calls=%async_computation.4 | async-start | bytes 737280 | tf_op jit(solution)/shard_map/reduce_scatter | solution.py:92
  176.0 269.3 %copy-start.5 = (s32[1,1,64]{2,1,0:T(1,128)S(1)}, s32[1,1,64]{2,1,0:T(1,128)}, u32[]{:S(2)}) copy-start(s32[1,1,64]{2,1,0:T(1,128)} %param.17) | copy-start | bytes 772
Sparse Core Ops, SparseCore 0:
  11.7 91.4 all-gather.2
  176.0 248.9 reduce-scatter.2
  445.4 33.5 reduce-scatter.4
where the time goes:
time: 489 us; the launch traced here: 488 us
  waiting for transfers between devices  357 us (73%)
  matrix products  67.7 us (14%)
  other arithmetic  23.6 us (5%)
  between operations  13.9 us (3%)
  blocking collectives  13.5 us (3%)
  local copies, waits for them, and re-layouts  11.6 us (2%)
    reduce_scatter x1, waiting for transfers between devices, shards(): lax.psum_scatter(jnp.concatenate([key_part, value_part], axis=1), 'ctx',...  240 us
    all_gather x1, waiting for transfers between devices, shards(): all_pairs = lax.all_gather(own_pair, 'ctx', axis=0, tiled=True)  85.1 us
    reduce_scatter x1, waiting for transfers between devices, shards(): lax.psum_scatter(jnp.dot(visual_grad, projector_weight, preferred_element...  32.2 us
    dot_general x1, matrix products, shards(): jnp.einsum('qhd,kd->hqk', grad_heads, value_all, preferred_element_type=j...  19.4 us
    all_gather x1, blocking collectives, shards(): lax.all_gather(chosen[None], ('section', 'dp'), axis=0, tiled=True)  13.5 us
    dot_general x1, matrix products, shards(): jnp.einsum('hqk,qhd->kd', probs_low, grad_heads, preferred_element_type=j...  13.4 us
    dot_general x1, matrix products, shards(): jnp.einsum('qhd,kd->hqk', query_heads, key_all, preferred_element_type=jn...  13.1 us
    reduce_sum x1, other arithmetic, shards(): summed = jnp.exp(masked_scores - running[:, :, None]).sum(axis=-1)  12.7 us
  transfers between devices with their start and end apart: 3, of which 3 were waited for; matrix products, arithmetic and copies ran while one was open for 4% of the time, Pallas kernels for 0%

commit v1 on v0

--- a/solution.py
+++ b/solution.py
@@ -33,7 +33,9 @@
     query_pos = query_first + jnp.arange(local_rows, dtype=jnp.int32)
     query_frames = lax.dynamic_slice_in_dim(frame_line, query_first, local_rows)
     own_pair = jnp.concatenate([key_vectors[0], value_vectors[0]], axis=1)
-    all_pairs = lax.all_gather(own_pair, "ctx", axis=0, tiled=True)
+    all_pairs = jnp.concatenate(
+        lax.all_to_all(jnp.stack([own_pair] * lax.axis_size("ctx")), "ctx", 0, 0), axis=0
+    )
     key_all = all_pairs[:, :HEAD_DIM]
     value_all = all_pairs[:, HEAD_DIM:]
     key_pos = jnp.arange(seq_total, dtype=jnp.int32)

time: 489 us -> 541 us (1.11)
  waiting for transfers between devices: 357 us -> 391 us
  starting transfers between devices: 0.12 us -> 16.9 us
    all_to_all x0 -> x1, waiting for transfers between devices: none -> 107 us  [shards(): lax.all_to_all(jnp.stack([own_pair] * lax.axis_size('ctx')), 'ctx', 0, 0)]
    all_gather x1 -> x0, waiting for transfers between devices: 85.1 us -> none  [shards(): all_pairs = lax.all_gather(own_pair, 'ctx', axis=0, tiled=True)]
    all_to_all x0 -> x1, starting transfers between devices: none -> 16.8 us  [shards(): lax.all_to_all(jnp.stack([own_pair] * lax.axis_size('ctx')), 'ctx', 0, 0)]
    reduce_scatter x1, waiting for transfers between devices: 240 us -> 251 us  [shards(): lax.psum_scatter(jnp.concatenate([key_part, value_part], axis=1), 'ctx',...]
where the time goes in v1:
time: 541 us; the launch traced here: 540 us
  waiting for transfers between devices  391 us (72%)
  matrix products  68 us (13%)
  other arithmetic  23 us (4%)
  starting transfers between devices  16.9 us (3%)
  between operations  14.2 us (3%)
  local copies, waits for them, and re-layouts  14 us (3%)
  blocking collectives  13.4 us (2%)
    reduce_scatter x1, waiting for transfers between devices, shards(): lax.psum_scatter(jnp.concatenate([key_part, value_part], axis=1), 'ctx',...  251 us
    all_to_all x1, waiting for transfers between devices, shards(): lax.all_to_all(jnp.stack([own_pair] * lax.axis_size('ctx')), 'ctx', 0, 0)  107 us
    reduce_scatter x1, waiting for transfers between devices, shards(): lax.psum_scatter(jnp.dot(visual_grad, projector_weight, preferred_element...  32.3 us
    dot_general x1, matrix products, shards(): jnp.einsum('qhd,kd->hqk', grad_heads, value_all, preferred_element_type=j...  19.8 us
    all_to_all x1, starting transfers between devices, shards(): lax.all_to_all(jnp.stack([own_pair] * lax.axis_size('ctx')), 'ctx', 0, 0)  16.8 us
    all_gather x1, blocking collectives, shards(): lax.all_gather(chosen[None], ('section', 'dp'), axis=0, tiled=True)  13.4 us
    dot_general x1, matrix products, shards(): jnp.einsum('hqk,qhd->kd', probs_low, grad_heads, preferred_element_type=j...  13.2 us
    dot_general x1, matrix products, shards(): jnp.einsum('qhd,kd->hqk', query_heads, key_all, preferred_element_type=jn...  13.1 us
  transfers between devices with their start and end apart: 3, of which 3 were waited for; matrix products, arithmetic and copies ran while one was open for 4% of the time, Pallas kernels for 0%

profile of v1, /device:TPU:8, one launch (start us, length us, event | category | flops | bytes accessed | tf_op | source)
XLA Modules:
  0.0 540.1 jit_solution(11632742201189067926)
XLA Ops:
  7.2 0.9 pad_maximum_fusion.2
  8.1 2.4 stack.2
  10.6 16.8 %all-to-all-start = ((bf16[64,128,256]{2,1,0:T(8,128)(2,1)}), bf16[64,128,256]{2,1,0:T(8,128)(2,1)}, u32[]{:S(2)}, u32[]{:S(2)}) async-start(bf16[64,128,256]{2,1,0:T(8,128)(2,1)} %stack.2), calls=%async_computation | async-start | bytes 8388608 | tf_op jit(solution)/shard_map/all_to_all | solution.py:37
  27.4 1.8 copy.28
  29.2 1.8 copy.26
  30.9 0.7 copy.50
  31.6 0.7 dynamic-slice_bitcast_fusion
  32.3 4.3 fusion.13
  36.6 107.3 %all-to-all-done = bf16[64,128,256]{2,1,0:T(8,128)(2,1)} async-done(((bf16[64,128,256]{2,1,0:T(8,128)(2,1)}), bf16[64,128,256]{2,1,0:T(8,128)(2,1)}, u32[]{:S(2)}, u32[]{:S(2)}) %all-to-all-start) | async-done | bytes 4194336 | tf_op jit(solution)/shard_map/all_to_all | solution.py:37
  143.9 13.1 %fusion.4 = (f32[7,128]{1,0:T(8,128)S(1)}, f32[8192,128,7]{1,0,2:T(8,128)}) fusion(pred[128,8192]{0,1:T(8,128)(4,1)S(1)} %fusion.13, bf16[128,7,128]{0,2,1:T(8,128)(2,1)} %bitcast.91, bf16[8192,256]{1,0:T(8,128)(2,1)} %bitcast.4), kind=kOutput, calls=%fused_computation.12 | convolution fusion | flops 1901067392 | bytes 32738816 | tf_op jit(solution)/shard_map/qhd,kd->hqk/dot_general | solution.py:46
  157.0 12.7 %exponential_reduce_fusion = f32[7,128]{1,0:T(8,128)S(1)} fusion(f32[8192,128,7]{1,0,2:T(8,128)} %get-tuple-element.14, f32[7,128]{1,0:T(8,128)S(1)} %get-tuple-element.13, pred[128,8192]{0,1:T(8,128)(4,1)S(1)} %fusion.13), kind=kLoop, calls=%fused_computation.11 | loop fusion | flops 29359232 | bytes 30415872 | tf_op jit(solution)/shard_map/reduce_sum | solution.py:51
  169.7 13.2 %fusion.9 = f32[8192,128]{0,1:T(8,128)S(1)} fusion(bf16[128,7,128]{0,2,1:T(8,128)(2,1)S(1)} %bitcast.93, f32[8192,128,7]{1,0,2:T(8,128)} %get-tuple-element.14, f32[7,128]{1,0:T(8,128)S(1)} %log_add_fusion, pred[128,8192]{0,1:T(8,128)(4,1)S(1)} %fusion.13), kind=kOutput, calls=%fused_computation.17 | convolution fusion | flops 1908408320 | bytes 34835968 | tf_op jit(solution)/shard_map/hqk,qhd->kd/dot_general | solution.py:67
  183.0 19.8 %fusion.1 = bf16[7,128,8192]{1,2,0:T(8,128)(2,1)} fusion(f32[8192,128,7]{1,0,2:T(8,128)} %get-tuple-element.14, bf16[128,7,128]{0,2,1:T(8,128)(2,1)S(1)} %bitcast.94, f32[7,128]{1,0:T(8,128)S(1)} %bitcast.99, f32[7,128]{1,0:T(8,128)S(1)} %log_add_fusion, pred[128,8192]{0,1:T(8,128)(4,1)S(1)} %fusion.13, bf16[8192,256]{1,0:T(8,128)(2,1)} %bitcast.4), kind=kOutput, calls=%fused_computation.6 | convolution fusion | flops 1923088384 | bytes 47422464 | tf_op jit(solution)/shard_map/qhd,kd->hqk/dot_general | solution.py:55
  202.8 9.9 %fusion.12 = f32[8192,128]{0,1:T(8,128)S(1)} fusion(bf16[7,128,8192]{1,2,0:T(8,128)(2,1)} %fusion.1, bf16[128,7,128]{0,2,1:T(8,128)(2,1)S(1)} %bitcast.92), kind=kOutput, calls=%fused_computation.18 | convolution fusion | flops 1880096768 | bytes 19103744 | tf_op jit(solution)/shard_map/hqk,qhd->kd/dot_general | solution.py:64
  212.7 4.1 pad_maximum_fusion
  217.0 8.2 %fusion.17 = bf16[128,7,128]{2,0,1:T(8,128)(2,1)S(1)} fusion(bf16[7,128,8192]{1,2,0:T(8,128)(2,1)} %fusion.1, bf16[8192,256]{1,0:T(8,128)(2,1)} %bitcast.4), kind=kOutput, calls=%fused_computation.28 | convolution fusion | flops 1879277568 | bytes 17006592 | tf_op jit(solution)/shard_map/hqk,kd->qhd/dot_general | solution.py:60
  225.2 0.2 copy.34
  225.3 0.6 gather_fusion
  226.0 250.9 %reduce-scatter.3.cloned.1.call-done = f32[128,256]{0,1:T(8,128)} async-done(((f32[8192,256]{0,1:T(8,128)}), f32[128,256]{0,1:T(8,128)}) %reduce-scatter.3.cloned.1.call-update) | async-done | bytes 131088 | tf_op jit(solution)/shard_map/reduce_scatter | solution.py:70
  476.9 0.9 convert.5
  477.8 0.1 copy.36
  477.9 0.6 gather_fusion.2
  478.5 0.1 copy.35
  478.6 0.6 gather_fusion.1
  479.3 13.4 %all-gather = bf16[256,1152]{1,0:T(8,128)(2,1)S(1)} all-gather(bf16[32,1152]{1,0:T(8,128)(2,1)S(1)} %pad_maximum_fusion.1), channel_id=2, replica_groups=mesh['ctx'=64,'section'=2,'dp'=4] {'section','dp'}, dimensions={0}, use_global_device_ids=true | all-gather | bytes 663552 | tf_op jit(solution)/shard_map/all_gather | solution.py:81
  492.7 0.6 copy.37
  493.4 3.7 convolution_convert_fusion
  497.2 0.7 copy.38
  497.9 0.7 copy.39
  498.6 32.3 %reduce-scatter.5.cloned.1.call-done = bf16[16,2560]{1,0:T(8,128)(2,1)} async-done(((bf16[128,2560]{1,0:T(8,128)(2,1)}), bf16[16,2560]{1,0:T(8,128)(2,1)}) %reduce-scatter.5.cloned.1.call-update) | async-done | bytes 81936 | tf_op jit(solution)/shard_map/reduce_scatter | solution.py:94
  530.9 0.9 reshape.161
  531.9 1.3 gather_fusion.3
  (23 shorter events, 0.3 us)
Async XLA Ops:
  7.2 486.2 %copy-start = (bf16[448,2560]{1,0:T(8,128)(2,1)S(1)}, bf16[448,2560]{1,0:T(8,128)(2,1)}, u32[]{:S(2)}) copy-start(bf16[448,2560]{1,0:T(8,128)(2,1)} %param.19) | copy-start | bytes 6881284
  10.6 133.3 %all-to-all-start = ((bf16[64,128,256]{2,1,0:T(8,128)(2,1)}), bf16[64,128,256]{2,1,0:T(8,128)(2,1)}, u32[]{:S(2)}, u32[]{:S(2)}) async-start(bf16[64,128,256]{2,1,0:T(8,128)(2,1)} %stack.2), calls=%async_computation | async-start | bytes 8388608 | tf_op jit(solution)/shard_map/all_to_all | solution.py:37
  27.3 449.5 %reduce-scatter.3.cloned.1.call-start = ((), (), s32[]{:S(2)}) async-start(), calls=%async_computation.3 | async-start | bytes 8519680 | tf_op jit(solution)/shard_map/reduce_scatter | solution.py:70
  157.0 12.7 %copy-start.2 = (bf16[1,128,896]{1,2,0:T(8,128)(2,1)S(1)}, bf16[1,128,896]{1,2,0:T(8,128)(2,1)}, u32[]{:S(2)}) copy-start(bf16[1,128,896]{1,2,0:T(8,128)(2,1)} %copy.28) | copy-start | bytes 688132
  183.0 19.8 %copy-start.1 = (bf16[1,128,896]{1,2,0:T(8,128)(2,1)S(1)}, bf16[1,128,896]{1,2,0:T(8,128)(2,1)}, u32[]{:S(2)}) copy-start(bf16[1,128,896]{1,2,0:T(8,128)(2,1)} %copy.26) | copy-start | bytes 688132
  212.7 4.2 copy-start.3
  216.9 314.1 %reduce-scatter.5.cloned.1.call-start = ((), (), s32[]{:S(2)}) async-start(), calls=%async_computation.4 | async-start | bytes 737280 | tf_op jit(solution)/shard_map/reduce_scatter | solution.py:94
  216.9 280.2 %copy-start.4 = (s32[1,1,64]{2,1,0:T(1,128)S(1)}, s32[1,1,64]{2,1,0:T(1,128)}, u32[]{:S(2)}) copy-start(s32[1,1,64]{2,1,0:T(1,128)} %param.17) | copy-start | bytes 772
Sparse Core Ops, SparseCore 0:
  217.0 259.8 reduce-scatter.2
  497.3 33.6 reduce-scatter.4
